TPU v7x, 128 devices: a whole 4x4x4 slice. The times are simulated.
128 devices in a mesh: src: 4 (over z), vol: 32 (over y, x, core).
Axes of the slice: x: 4, y: 4, z: 4, core: 2. Of those that a mesh axis runs over, the one named last changes fastest.
Arguments:
- forward: bfloat16 [16384, 36, 512], P(('src', 'vol')), may hold values from -6 to 6
- item_tx: int32 [16384], P(('src', 'vol')), may hold values from 0 to 15, as said below
- item_brick: int32 [16384], P(('src', 'vol')), may hold values from 0 to 1023
- tx_place: int32 [16], replicated, may hold values from 0 to 15, as said below
- brick_place: int32 [1024], replicated, may hold values from 0 to 1023, as said below
- adjoint: bfloat16 [16, 1024, 36, 512], P('src', 'vol'), may hold values from -6 to 6
Outputs:
- gradient: float32 [2, 256, 16, 128], P(None, 'vol')
Inputs may be any that keep to these rules, and one draw needn't show every extreme that they name: Stored brick i goes to owner (tx_place[item_tx[i]] // 4, brick_place[item_brick[i]] // 32) as (src index, vol index). Among the stored bricks of one device at most 2 share an owner; in every draw one owner receives exactly 2 from every device. `tx_place`: A permutation. `brick_place`: A permutation.
All inputs are finite; a program needn't handle non-finite values.
Results may differ from a plain program's by a relative error of at most 0.0003.
Values may be sent and summed in bfloat16 or wider, within the bound.
No kernel may reach another device: no remote copies, remote signals or barrier semaphores. Data moves between devices by JAX's collectives and lax.ppermute only.
A program may use at most 128 MiB of HBM per device.

v0:
```python
import math
import jax
import jax.numpy as jnp
from jax import lax
from jax.sharding import PartitionSpec as P

E = 8
NFREQ = 6
NBY = 2
NBZ = 16


def with_halo(cells, sides, width):
    for axis, dim in sides:
        count = lax.axis_size(axis)
        ends = count - 1
        head = lax.slice_in_dim(cells, 0, width, axis=dim)
        tail = lax.slice_in_dim(cells, cells.shape[dim] - width, cells.shape[dim], axis=dim)
        cells = jnp.concatenate(
            [
                lax.ppermute(tail, axis, [(i, (i + 1) % count) for i in range(ends)]),
                cells,
                lax.ppermute(head, axis, [((i + 1) % count, i) for i in range(ends)]),
            ],
            axis=dim,
        )
    return cells


def tap_weights():
    raw_taps = [math.exp(-(offset - 4) * (offset - 4) / 4.5) for offset in range(9)]
    tap_total = sum(raw_taps)
    return [tap_value / tap_total for tap_value in raw_taps]


def correlate(fwd_field, adj_field):
    lead_shape = fwd_field.shape[:-2]
    fwd_split = fwd_field.reshape(lead_shape + (NFREQ, 3, 2, fwd_field.shape[-1]))
    adj_split = adj_field.reshape(lead_shape + (NFREQ, 3, 2, adj_field.shape[-1]))
    products = (
        fwd_split[..., 0, :] * adj_split[..., 0, :] - fwd_split[..., 1, :] * adj_split[..., 1, :]
    )
    horizontal = jnp.sum(products[..., 0:2, :], axis=(-3, -2))
    vertical = jnp.sum(products[..., 2, :], axis=-2)
    return jnp.stack([horizontal, vertical], axis=-2)


def smooth_axis(padded, axis):
    weights = tap_weights()
    length = padded.shape[axis] - 8
    summed = jnp.zeros(padded.shape[:axis] + (length,) + padded.shape[axis + 1 :], jnp.float32)
    for offset in range(9):
        summed = summed + weights[offset] * lax.slice_in_dim(
            padded, offset, offset + length, axis=axis
        )
    return summed


def pad_axis(field, axis):
    widths = [(0, 0)] * field.ndim
    widths[axis] = (4, 4)
    return jnp.pad(field, widths)


def lookup(indices, table):
    hits = indices[:, None] == jnp.arange(table.shape[0], dtype=jnp.int32)[None, :]
    return jnp.sum(jnp.where(hits, table[None, :], 0), axis=1)


def local(forward, item_tx, item_brick, tx_place, brick_place, adjoint):
    stored = forward.shape[0]
    channels = forward.shape[1]
    cells = forward.shape[2]
    src_count = lax.axis_size("src")
    vol_count = lax.axis_size("vol")
    devices = src_count * vol_count
    local_tx = adjoint.shape[0]
    local_bricks = adjoint.shape[1]
    capacity = max(2, 2 * stored // devices)
    slot_total = devices * capacity
    tx_at = lookup(item_tx, tx_place)
    brick_at = lookup(item_brick, brick_place)
    destination = tx_at // local_tx * vol_count + brick_at // local_bricks
    pair_index = tx_at % local_tx * local_bricks + brick_at % local_bricks
    positions = jnp.arange(stored, dtype=jnp.int32)
    same_owner = destination[:, None] == destination[None, :]
    earlier = positions[:, None] > positions[None, :]
    order_rank = jnp.sum((same_owner & earlier).astype(jnp.int32), axis=1)
    slot_index = destination * capacity + order_rank
    outgoing = jnp.zeros((slot_total, channels, cells), forward.dtype).at[slot_index].set(forward)
    slot_pairs = jnp.full((slot_total,), -1, jnp.int32).at[slot_index].set(pair_index)
    arrived, arrived_pairs = (
        lax.all_to_all(outgoing, ("src", "vol"), split_axis=0, concat_axis=0, tiled=True),
        lax.all_to_all(slot_pairs, ("src", "vol"), split_axis=0, concat_axis=0, tiled=True),
    )
    filled = arrived_pairs >= 0
    flat_adjoint = adjoint.reshape(local_tx * local_bricks, channels, cells)
    picked = flat_adjoint[jnp.maximum(arrived_pairs, 0)]
    product = correlate(arrived.astype(jnp.float32), picked.astype(jnp.float32))
    owner_brick = arrived_pairs % local_bricks
    owner_table = (
        (owner_brick[None, :] == jnp.arange(local_bricks, dtype=jnp.int32)[:, None])
        & filled[None, :]
    ).astype(jnp.float32)
    gradient = jnp.dot(
        owner_table, product.reshape(slot_total, 2 * cells), precision=lax.Precision.HIGHEST
    )
    gradient = gradient.reshape(local_bricks, 2, cells)
    slab = (
        gradient.reshape(NBY, NBZ, 2, E, E, E)
        .transpose(2, 3, 0, 4, 1, 5)
        .reshape(2, E, NBY * E, NBZ * E)
    )
    summed = lax.psum(slab, "src")
    padded = with_halo(summed, (("vol", 1),), 4)
    field = smooth_axis(padded, 1)
    for axis in (2, 3):
        field = smooth_axis(pad_axis(field, axis), axis)
    return field


def solution(mesh):
    in_specs = (
        P(("src", "vol"), None, None),
        P(("src", "vol")),
        P(("src", "vol")),
        P(),
        P(),
        P("src", "vol", None, None),
    )
    out_specs = P(None, "vol", None, None)
    return jax.shard_map(local, mesh=mesh, in_specs=in_specs, out_specs=out_specs, check_vma=False)
```

profile of v0, /device:TPU:7, one launch (start us, length us, event | category | flops | bytes accessed | tf_op | source)
XLA Modules:
  0.0 298.9 jit_solution(5812231663383494735)
XLA Ops:
  6.5 0.8 select_reduce_fusion.1
  7.3 0.9 select_reduce_fusion
  8.4 1.0 scatter_custom_fusion
  9.4 0.8 all_to_all.11
  10.2 10.8 %all-to-all-start = ((s32[128,2,1]{1,2,0:T(1,128)}), s32[128,2,1]{1,2,0:T(1,128)S(1)}, u32[]{:S(2)}, u32[]{:S(2)}) async-start(s32[128,2,1]{1,2,0:T(1,128)} %bitcast.4), calls=%async_computation | async-start | bytes 131072 | tf_op jit(solution)/shard_map/all_to_all | solution.py:94
  21.0 7.3 %copy.49 = bf16[128,36,512]{2,1,0:T(8,128)(2,1)} copy(bf16[128,36,512]{2,0,1:T(8,128)(2,1)} %param.6) | data formatting | bytes 9437184 | tf_op args[0]
  28.3 4.6 %broadcast_in_dim.33 = bf16[256,36,512]{2,1,0:T(8,128)(2,1)} broadcast(bf16[]{:T(256)} %constant.76.clone.1), dimensions={} | broadcast | bytes 9437186 | tf_op jit(solution)/shard_map/broadcast_in_dim | solution.py:90
  32.8 20.5 %scatter_fusion = bf16[256,36,512]{2,1,0:T(8,128)(2,1)} fusion(bf16[256,36,512]{2,1,0:T(8,128)(2,1)} %broadcast_in_dim.33, s32[128]{0:T(128)S(1)} %fusion.52, bf16[128,36,512]{2,1,0:T(8,128)(2,1)} %copy.49), kind=kCustom, calls=%fused_computation.2 | custom fusion | bytes 14156288 | tf_op jit(solution)/shard_map/scatter | solution.py:90
  53.4 10.3 %all-to-all-start.1 = ((bf16[256,36,512]{2,1,0:T(8,128)(2,1)}), bf16[256,36,512]{2,1,0:T(8,128)(2,1)}, u32[]{:S(2)}, u32[]{:S(2)}) async-start(bf16[256,36,512]{2,1,0:T(8,128)(2,1)} %scatter_fusion), calls=%async_computation.1 | async-start | bytes 20971520 | tf_op jit(solution)/shard_map/all_to_all | solution.py:93
  63.9 2.7 copy.51
  66.6 5.1 %copy.52 = bf16[128,36,512]{2,1,0:T(8,128)(2,1)} copy(bf16[128,36,512]{2,0,1:T(8,128)(2,1)S(1)} %bitcast.58) | data formatting | bytes 9437184 | tf_op jit(solution)/shard_map/reshape | solution.py:97
  71.7 0.5 broadcast.393
  72.2 1.0 fusion.55
  73.5 12.1 %gather_fusion = bf16[256,36,512]{2,1,0:T(8,128)(2,1)} fusion(bf16[128,36,512]{2,1,0:T(8,128)(2,1)} %copy.52, s32[1024]{0:T(1024)S(1)} %pad_clamp_fusion), kind=kCustom, calls=%fused_computation | custom fusion | bytes 18875392 | tf_op jit(solution)/shard_map/gather | solution.py:98
  85.6 10.9 %copy.53 = bf16[256,36,512]{2,0,1:T(8,128)(2,1)} copy(bf16[256,36,512]{2,1,0:T(8,128)(2,1)} %gather_fusion) | data formatting | bytes 18874368 | tf_op jit(solution)/shard_map/gather | solution.py:98
  96.5 12.7 %convert.3 = f32[256,6,3,2,512]{4,0,3,2,1:T(8,128)} convert(bf16[256,6,3,2,512]{4,0,3,2,1:T(8,128)(2,1)} %bitcast.56) | non-fusion elementwise | flops 4718592 | bytes 28311552 | tf_op jit(solution)/shard_map/convert_element_type | solution.py:99
  109.2 77.3 %all-to-all-done.1 = bf16[256,36,512]{2,1,0:T(8,128)(2,1)} async-done(((bf16[256,36,512]{2,1,0:T(8,128)(2,1)}), bf16[256,36,512]{2,1,0:T(8,128)(2,1)}, u32[]{:S(2)}, u32[]{:S(2)}) %all-to-all-start.1) | async-done | bytes 9437216 | tf_op jit(solution)/shard_map/all_to_all | solution.py:93
  186.5 10.9 %copy.50 = bf16[256,36,512]{2,0,1:T(8,128)(2,1)} copy(bf16[256,36,512]{2,1,0:T(8,128)(2,1)} %all-to-all-done.1) | data formatting | bytes 18874368 | tf_op jit(solution)/shard_map/all_to_all | solution.py:93
  197.4 12.7 %convert.2 = f32[256,6,3,2,512]{4,0,3,2,1:T(8,128)} convert(bf16[256,6,3,2,512]{4,0,3,2,1:T(8,128)(2,1)} %bitcast.57) | non-fusion elementwise | flops 4718592 | bytes 28311552 | tf_op jit(solution)/shard_map/reshape | solution.py:38
  210.1 14.0 %fusion.1 = f32[256,6,3,512]{3,0,2,1:T(8,128)S(1)} fusion(f32[256,6,3,2,512]{4,0,3,2,1:T(8,128)} %convert.3, f32[256,6,3,2,512]{4,0,3,2,1:T(8,128)} %convert.2), kind=kLoop, calls=%fused_computation.5 | loop fusion | flops 7077888 | bytes 47185920 | tf_op jit(solution)/shard_map/sub | solution.py:41
  224.5 0.7 slice_reduce_fusion
  225.7 0.7 convolution_bitcast_fusion
  226.4 0.6 copy.55
  227.0 1.6 reshape.258
  228.7 46.9 %all-reduce.4.cloned.1.call-done = f32[2,8,16,128]{3,2,1,0:T(8,128)} async-done(((f32[2,8,16,128]{3,2,1,0:T(8,128)}), f32[2,8,16,128]{3,2,1,0:T(8,128)}) %all-reduce.4.cloned.1.call-update) | async-done | bytes 131088 | tf_op jit(solution)/shard_map/psum | solution.py:114
  275.6 0.9 fusion.56
  276.5 5.7 %collective-permute-start = (f32[2,4,16,128]{3,2,1,0:T(8,128)S(1)}, f32[2,4,16,128]{3,2,1,0:T(8,128)S(1)}, u32[]{:S(2)}, u32[]{:S(2)}) collective-permute-start(f32[2,4,16,128]{3,2,1,0:T(8,128)S(1)} %get-tuple-element.9), channel_id=1, source_target_pairs={{0,1},{1,2},{2,3},{3,4},{4,5},{5,6},{6,7},{7,8},{8,9},{9,10},{10,1... | collective-permute-start | bytes 196616 | tf_op jit(solution)/shard_map/ppermute | solution.py:21
  282.2 1.9 collective-permute-start.1
  284.1 0.9 constant_dynamic-update-slice_fusion
  285.1 4.8 %collective-permute-done.1 = f32[2,4,16,128]{3,2,1,0:T(8,128)S(1)} collective-permute-done((f32[2,4,16,128]{3,2,1,0:T(8,128)S(1)}, f32[2,4,16,128]{3,2,1,0:T(8,128)S(1)}, u32[]{:S(2)}, u32[]{:S(2)}) %collective-permute-start.1) | collective-permute-done | bytes 65568 | tf_op jit(solution)/shard_map/ppermute | solution.py:23
  289.9 1.0 fusion.34
  291.0 1.0 fusion.26
  (19 shorter events, 1.7 us)
Async XLA Ops:
  10.2 43.2 %all-to-all-start = ((s32[128,2,1]{1,2,0:T(1,128)}), s32[128,2,1]{1,2,0:T(1,128)S(1)}, u32[]{:S(2)}, u32[]{:S(2)}) async-start(s32[128,2,1]{1,2,0:T(1,128)} %bitcast.4), calls=%async_computation | async-start | bytes 131072 | tf_op jit(solution)/shard_map/all_to_all | solution.py:94
  53.4 133.2 %all-to-all-start.1 = ((bf16[256,36,512]{2,1,0:T(8,128)(2,1)}), bf16[256,36,512]{2,1,0:T(8,128)(2,1)}, u32[]{:S(2)}, u32[]{:S(2)}) async-start(bf16[256,36,512]{2,1,0:T(8,128)(2,1)} %scatter_fusion), calls=%async_computation.1 | async-start | bytes 20971520 | tf_op jit(solution)/shard_map/all_to_all | solution.py:93
  63.6 211.9 %all-reduce.4.cloned.1.call-start = ((), (), s32[]{:S(2)}) async-start(), calls=%async_computation.2 | async-start | bytes 262144 | tf_op jit(solution)/shard_map/psum | solution.py:114
  276.5 7.7 %collective-permute-start = (f32[2,4,16,128]{3,2,1,0:T(8,128)S(1)}, f32[2,4,16,128]{3,2,1,0:T(8,128)S(1)}, u32[]{:S(2)}, u32[]{:S(2)}) collective-permute-start(f32[2,4,16,128]{3,2,1,0:T(8,128)S(1)} %get-tuple-element.9), channel_id=1, source_target_pairs={{0,1},{1,2},{2,3},{3,4},{4,5},{5,6},{6,7},{7,8},{8,9},{9,10},{10,1... | collective-permute-start | bytes 196616 | tf_op jit(solution)/shard_map/ppermute | solution.py:21
  282.2 7.7 %collective-permute-start.1 = (f32[2,4,16,128]{3,2,1,0:T(8,128)S(1)}, f32[2,4,16,128]{3,2,1,0:T(8,128)S(1)}, u32[]{:S(2)}, u32[]{:S(2)}) collective-permute-start(f32[2,4,16,128]{3,2,1,0:T(8,128)S(1)} %get-tuple-element.10), channel_id=1, source_target_pairs={{1,0},{2,1},{3,2},{4,3},{5,4},{6,5},{7,6},{8,7},{9,8},{10,9},{11,1... | collective-permute-start | bytes 196616 | tf_op jit(solution)/shard_map/ppermute | solution.py:23
Sparse Core Ops, SparseCore 0:
  228.8 46.7 all-reduce.3
where the time goes:
time: 300 us; the launch traced here: 299 us
  waiting for transfers between devices  129 us (43%)
  local copies, waits for them, and re-layouts  81 us (27%)
  other arithmetic  45.6 us (15%)
  starting transfers between devices  28.9 us (10%)
  between operations  13.6 us (5%)
    all_to_all x1, waiting for transfers between devices, local(): lax.all_to_all(outgoing, ('src', 'vol'), split_axis=0, concat_axis=0, til...  77.3 us
    psum x1, waiting for transfers between devices, local(): summed = lax.psum(slab, 'src')  46.9 us
    gather x2, local copies, waits for them, and re-layouts, local(): picked = flat_adjoint[jnp.maximum(arrived_pairs, 0)]  23 us
    scatter x1, local copies, waits for them, and re-layouts, local(): jnp.zeros((slot_total, channels, cells), forward.dtype).at[slot_index]  20.5 us
    sub x1, other arithmetic, correlate(): fwd_split[..., 0, :] * adj_split[..., 0, :]  14 us
    convert_element_type x1, other arithmetic, local(): product = correlate(arrived.astype(jnp.float32), picked.astype(jnp.float32))  12.7 us
    reshape x1, other arithmetic, correlate(): fwd_field.reshape(lead_shape + (NFREQ, 3, 2, fwd_field.shape[-1]))  12.7 us
    all_to_all x1, local copies, waits for them, and re-layouts, local(): lax.all_to_all(outgoing, ('src', 'vol'), split_axis=0, concat_axis=0, til...  10.9 us
  transfers between devices with their start and end apart: 5, of which 3 were waited for; matrix products, arithmetic and copies ran while one was open for 26% of the time, Pallas kernels for 0%

commit v1 on v0

--- a/solution.py
+++ b/solution.py
@@ -111,7 +111,7 @@
         .transpose(2, 3, 0, 4, 1, 5)
         .reshape(2, E, NBY * E, NBZ * E)
     )
-    summed = lax.psum(slab, "src")
+    summed = jnp.sum(lax.all_gather(slab, "src"), axis=0)
     padded = with_halo(summed, (("vol", 1),), 4)
     field = smooth_axis(padded, 1)
     for axis in (2, 3):

time: 300 us -> 254 us (0.85)
  the two profiles are of different devices: /device:TPU:7 before, /device:TPU:1 now
where the time goes in v1:
time: 254 us; the launch traced here: 253 us
  waiting for transfers between devices  81.7 us (32%)
  local copies, waits for them, and re-layouts  78.6 us (31%)
  other arithmetic  44.8 us (18%)
  starting transfers between devices  34.7 us (14%)
  blocking collectives  12.8 us (5%)
    all_to_all x1, waiting for transfers between devices, local(): lax.all_to_all(outgoing, ('src', 'vol'), split_axis=0, concat_axis=0, til...  78 us
    gather x2, local copies, waits for them, and re-layouts, local(): picked = flat_adjoint[jnp.maximum(arrived_pairs, 0)]  23 us
    scatter x1, local copies, waits for them, and re-layouts, local(): jnp.zeros((slot_total, channels, cells), forward.dtype).at[slot_index]  20.5 us
    sub x1, other arithmetic, correlate(): fwd_split[..., 0, :] * adj_split[..., 0, :]  14 us
    all_gather x1, blocking collectives, local(): summed = jnp.sum(lax.all_gather(slab, 'src'), axis=0)  12.8 us
    convert_element_type x1, other arithmetic, local(): product = correlate(arrived.astype(jnp.float32), picked.astype(jnp.float32))  12.7 us
    reshape x1, other arithmetic, correlate(): fwd_field.reshape(lead_shape + (NFREQ, 3, 2, fwd_field.shape[-1]))  12.7 us
    all_to_all x1, starting transfers between devices, local(): lax.all_to_all(slot_pairs, ('src', 'vol'), split_axis=0, concat_axis=0, t...  11.5 us
  transfers between devices with their start and end apart: 4, of which 2 were waited for; matrix products, arithmetic and copies ran while one was open for 31% of the time, Pallas kernels for 0%

profile of v1, /device:TPU:1, one launch (start us, length us, event | category | flops | bytes accessed | tf_op | source)
XLA Modules:
  0.0 253.3 jit_solution(1560636271729991520)
XLA Ops:
  0.0 0.8 select_reduce_fusion.1
  0.8 0.9 select_reduce_fusion
  1.7 0.2 convert_reduce_fusion
  1.9 1.0 scatter_custom_fusion
  2.9 0.8 all_to_all.11
  3.6 11.5 %all-to-all-start = ((s32[128,2,1]{1,2,0:T(1,128)}), s32[128,2,1]{1,2,0:T(1,128)S(1)}, u32[]{:S(2)}, u32[]{:S(2)}) async-start(s32[128,2,1]{1,2,0:T(1,128)} %bitcast.4), calls=%async_computation | async-start | bytes 131072 | tf_op jit(solution)/shard_map/all_to_all | solution.py:94
  15.1 7.3 %copy.49 = bf16[128,36,512]{2,1,0:T(8,128)(2,1)} copy(bf16[128,36,512]{2,0,1:T(8,128)(2,1)} %param.6) | data formatting | bytes 9437184 | tf_op args[0]
  22.5 4.6 %broadcast_in_dim.33 = bf16[256,36,512]{2,1,0:T(8,128)(2,1)} broadcast(bf16[]{:T(256)} %constant.76.clone.1), dimensions={} | broadcast | bytes 9437186 | tf_op jit(solution)/shard_map/broadcast_in_dim | solution.py:90
  27.0 20.5 %scatter_fusion = bf16[256,36,512]{2,1,0:T(8,128)(2,1)} fusion(bf16[256,36,512]{2,1,0:T(8,128)(2,1)} %broadcast_in_dim.33, s32[128]{0:T(128)S(1)} %fusion.66, bf16[128,36,512]{2,1,0:T(8,128)(2,1)} %copy.49), kind=kCustom, calls=%fused_computation.2 | custom fusion | bytes 14156288 | tf_op jit(solution)/shard_map/scatter | solution.py:90
  47.5 10.3 %all-to-all-start.1 = ((bf16[256,36,512]{2,1,0:T(8,128)(2,1)}), bf16[256,36,512]{2,1,0:T(8,128)(2,1)}, u32[]{:S(2)}, u32[]{:S(2)}) async-start(bf16[256,36,512]{2,1,0:T(8,128)(2,1)} %scatter_fusion), calls=%async_computation.1 | async-start | bytes 20971520 | tf_op jit(solution)/shard_map/all_to_all | solution.py:93
  57.8 2.7 %copy.51 = bf16[4,32,36,512]{3,1,0,2:T(8,128)(2,1)S(1)} copy(bf16[4,32,36,512]{3,1,2,0:T(8,128)(2,1)} %param.11) | data formatting | bytes 9437184 | tf_op args[5]
  60.5 5.1 %copy.52 = bf16[128,36,512]{2,1,0:T(8,128)(2,1)} copy(bf16[128,36,512]{2,0,1:T(8,128)(2,1)S(1)} %bitcast.58) | data formatting | bytes 9437184 | tf_op jit(solution)/shard_map/reshape | solution.py:97
  65.6 0.5 broadcast.393
  66.1 1.0 fusion.69
  67.4 12.1 %gather_fusion = bf16[256,36,512]{2,1,0:T(8,128)(2,1)} fusion(bf16[128,36,512]{2,1,0:T(8,128)(2,1)} %copy.52, s32[1024]{0:T(1024)S(1)} %pad_clamp_fusion), kind=kCustom, calls=%fused_computation | custom fusion | bytes 18875392 | tf_op jit(solution)/shard_map/gather | solution.py:98
  79.5 10.9 %copy.53 = bf16[256,36,512]{2,0,1:T(8,128)(2,1)} copy(bf16[256,36,512]{2,1,0:T(8,128)(2,1)} %gather_fusion) | data formatting | bytes 18874368 | tf_op jit(solution)/shard_map/gather | solution.py:98
  90.4 12.7 %convert.3 = f32[256,6,3,2,512]{4,0,3,2,1:T(8,128)} convert(bf16[256,6,3,2,512]{4,0,3,2,1:T(8,128)(2,1)} %bitcast.56) | non-fusion elementwise | flops 4718592 | bytes 28311552 | tf_op jit(solution)/shard_map/convert_element_type | solution.py:99
  103.2 78.0 %all-to-all-done.1 = bf16[256,36,512]{2,1,0:T(8,128)(2,1)} async-done(((bf16[256,36,512]{2,1,0:T(8,128)(2,1)}), bf16[256,36,512]{2,1,0:T(8,128)(2,1)}, u32[]{:S(2)}, u32[]{:S(2)}) %all-to-all-start.1) | async-done | bytes 9437216 | tf_op jit(solution)/shard_map/all_to_all | solution.py:93
  181.2 10.9 %copy.50 = bf16[256,36,512]{2,0,1:T(8,128)(2,1)} copy(bf16[256,36,512]{2,1,0:T(8,128)(2,1)} %all-to-all-done.1) | data formatting | bytes 18874368 | tf_op jit(solution)/shard_map/all_to_all | solution.py:93
  192.1 12.7 %convert.2 = f32[256,6,3,2,512]{4,0,3,2,1:T(8,128)} convert(bf16[256,6,3,2,512]{4,0,3,2,1:T(8,128)(2,1)} %bitcast.57) | non-fusion elementwise | flops 4718592 | bytes 28311552 | tf_op jit(solution)/shard_map/reshape | solution.py:38
  204.8 14.0 %fusion.1 = f32[256,6,3,512]{3,0,2,1:T(8,128)S(1)} fusion(f32[256,6,3,2,512]{4,0,3,2,1:T(8,128)} %convert.3, f32[256,6,3,2,512]{4,0,3,2,1:T(8,128)} %convert.2), kind=kLoop, calls=%fused_computation.5 | loop fusion | flops 7077888 | bytes 47185920 | tf_op jit(solution)/shard_map/sub | solution.py:41
  218.8 0.4 slice_reduce_fusion.1
  219.2 0.7 slice_reduce_fusion
  220.0 0.3 copy.54
  220.4 0.7 convolution_bitcast_fusion
  221.0 0.6 copy.55
  221.7 1.0 all_gather_reshape.3
  222.7 12.8 %all_gather.3 = f32[4,2,8,16,128]{4,3,2,1,0:T(8,128)S(1)} all-gather(f32[1,2,8,16,128]{4,3,2,1,0:T(8,128)S(1)} %all_gather_reshape.3), channel_id=1, replica_groups=mesh['src'=4,'vol'=32] {'src'}, dimensions={0}, use_global_device_ids=true | all-gather | bytes 655360 | tf_op jit(solution)/shard_map/all_gather | solution.py:114
  235.5 11.0 %collective-permute-start = (f32[2,4,16,128]{3,2,1,0:T(8,128)S(1)}, f32[2,4,16,128]{3,2,1,0:T(8,128)S(1)}, u32[]{:S(2)}, u32[]{:S(2)}) collective-permute-start(f32[2,4,16,128]{3,2,1,0:T(8,128)S(1)} %get-tuple-element.7), channel_id=1, source_target_pairs={{0,1},{1,2},{2,3},{3,4},{4,5},{5,6},{6,7},{7,8},{8,9},{9,10},{10,1... | collective-permute-start | bytes 196616 | tf_op jit(solution)/shard_map/ppermute | solution.py:21
  246.5 1.9 collective-permute-start.1
  248.5 3.6 %collective-permute-done.1 = f32[2,4,16,128]{3,2,1,0:T(8,128)S(1)} collective-permute-done((f32[2,4,16,128]{3,2,1,0:T(8,128)S(1)}, f32[2,4,16,128]{3,2,1,0:T(8,128)S(1)}, u32[]{:S(2)}, u32[]{:S(2)}) %collective-permute-start.1) | collective-permute-done | bytes 65568 | tf_op jit(solution)/shard_map/ppermute | solution.py:23
  252.3 1.0 fusion.46
  (15 shorter events, 0.7 us)
Async XLA Ops:
  3.6 43.9 %all-to-all-start = ((s32[128,2,1]{1,2,0:T(1,128)}), s32[128,2,1]{1,2,0:T(1,128)S(1)}, u32[]{:S(2)}, u32[]{:S(2)}) async-start(s32[128,2,1]{1,2,0:T(1,128)} %bitcast.4), calls=%async_computation | async-start | bytes 131072 | tf_op jit(solution)/shard_map/all_to_all | solution.py:94
  47.5 133.7 %all-to-all-start.1 = ((bf16[256,36,512]{2,1,0:T(8,128)(2,1)}), bf16[256,36,512]{2,1,0:T(8,128)(2,1)}, u32[]{:S(2)}, u32[]{:S(2)}) async-start(bf16[256,36,512]{2,1,0:T(8,128)(2,1)} %scatter_fusion), calls=%async_computation.1 | async-start | bytes 20971520 | tf_op jit(solution)/shard_map/all_to_all | solution.py:93
  235.5 12.9 %collective-permute-start = (f32[2,4,16,128]{3,2,1,0:T(8,128)S(1)}, f32[2,4,16,128]{3,2,1,0:T(8,128)S(1)}, u32[]{:S(2)}, u32[]{:S(2)}) collective-permute-start(f32[2,4,16,128]{3,2,1,0:T(8,128)S(1)} %get-tuple-element.7), channel_id=1, source_target_pairs={{0,1},{1,2},{2,3},{3,4},{4,5},{5,6},{6,7},{7,8},{8,9},{9,10},{10,1... | collective-permute-start | bytes 196616 | tf_op jit(solution)/shard_map/ppermute | solution.py:21
  246.5 5.6 %collective-permute-start.1 = (f32[2,4,16,128]{3,2,1,0:T(8,128)S(1)}, f32[2,4,16,128]{3,2,1,0:T(8,128)S(1)}, u32[]{:S(2)}, u32[]{:S(2)}) collective-permute-start(f32[2,4,16,128]{3,2,1,0:T(8,128)S(1)} %get-tuple-element.8), channel_id=1, source_target_pairs={{1,0},{2,1},{3,2},{4,3},{5,4},{6,5},{7,6},{8,7},{9,8},{10,9},{11,1... | collective-permute-start | bytes 196616 | tf_op jit(solution)/shard_map/ppermute | solution.py:23
